TPU v7x, 128 devices: a whole 4x4x4 slice. The times are simulated.
128 devices in a mesh: dp: 4 (over x), seq: 8 (over z, core), expert: 4 (over y).
Axes of the slice: x: 4, y: 4, z: 4, core: 2. Of those that a mesh axis runs over, the one named last changes fastest.
Arguments:
- x_in: bfloat16 [4096, 8192], P(('dp', 'seq'), 'expert'), parts along dimension 0, may hold values from -6 to 6
- z_in: bfloat16 [4096, 8192], P(('dp', 'seq'), 'expert'), parts along dimension 0, may hold values from -6 to 6
- step_raw: bfloat16 [4096, 8192], P(('dp', 'seq'), 'expert'), parts along dimension 0, may hold values from -4 to 4
- step_bias: float32 [8192], P('expert'), may hold values from -9 to -2
- decay_rate: float32 [16, 8192], P(None, 'expert'), may hold values from 0.5 to 4
- b_coef: bfloat16 [16, 4096], P(None, ('dp', 'seq')), parts along dimension 1, may hold values from -6 to 6
- c_coef: bfloat16 [16, 4096], P(None, ('dp', 'seq')), parts along dimension 1, may hold values from -6 to 6
- skip_gain: float32 [8192], P('expert'), may hold values from 0.5 to 1.5
- out_proj: bfloat16 [8192, 8192], P('expert', 'seq'), may hold values from -0.0625 to 0.0625
- residual: bfloat16 [4096, 8192], P(('dp', 'seq', 'expert')), parts along dimension 0, may hold values from -6 to 6
- norm_gain: float32 [8192], replicated, may hold values from 0.5 to 1.5
- router_weight: bfloat16 [8192, 16], replicated, may hold values from -0.0625 to 0.0625
- expert_ids: int32 [4096, 2], P(('dp', 'seq', 'expert')), parts along dimension 0, may hold values from 0 to 15, as said below
- gate_weight: bfloat16 [8192, 12288], P(None, ('seq', 'expert')), may hold values from -0.0625 to 0.0625
- up_weight: bfloat16 [8192, 12288], P(None, ('seq', 'expert')), may hold values from -0.0625 to 0.0625
- down_weight: bfloat16 [12288, 8192], P(('seq', 'expert')), may hold values from -0.0546875 to 0.0546875
Outputs:
- final: bfloat16 [4096, 8192], P(('dp', 'seq', 'expert')), parts along dimension 0
There are 4 independent parts, one for each index of `dp`. A program takes and returns all parts, laid end to end along the dimension named above; an argument that names none is the same for every part. Nothing has to cross between parts.
Inputs may be any that keep to these rules, and one draw needn't show every extreme that they name: `expert_ids`: each token names 2 different experts; among the 32 rows of one device at most 16 name expert 0 and at least one does; on some device exactly 16 do.
All inputs are finite; a program needn't handle non-finite values.
Results may differ from a plain program's by a relative error of at most 0.006.
Values may be sent and summed in bfloat16 or wider, within the bound.
No kernel may reach another device: no remote copies, remote signals or barrier semaphores. Data moves between devices by JAX's collectives and lax.ppermute only.
A program may use at most 192 MiB of HBM per device.

v0:
```python
import jax
import jax.numpy as jnp
from jax import lax
from jax.sharding import PartitionSpec as P

BLOCK = 128


def entering(value, axis, join, neutral):
    count, mine = (lax.axis_size(axis), lax.axis_index(axis))
    pieces = jax.tree.map(lambda part: lax.all_gather(part, axis), value)
    running = jax.tree.map(
        lambda part, zero: jnp.full_like(part, 0) + jnp.asarray(zero, part.dtype), value, neutral
    )

    def hop(position, running):
        longer = join(running, jax.tree.map(lambda part: part[position], pieces))
        return jax.tree.map(lambda new, old: jnp.where(position < mine, new, old), longer, running)

    return lax.fori_loop(0, count - 1, hop, running)


def pair_combine(early, later):
    return (early[0] * later[0], later[0] * early[1] + later[1])


def end_state(step_size, x_float, decay_rate, b_rows):

    def end_advance(state, inputs):
        step_now, x_now, b_now = inputs
        state = (
            jnp.exp(-step_now[None, :] * decay_rate) * state
            + (step_now * x_now)[None, :] * b_now[:, None]
        )
        return (state, None)

    start_state = jnp.zeros(decay_rate.shape, jnp.float32)
    final_state, _ = lax.scan(end_advance, start_state, (step_size, x_float, b_rows), unroll=8)
    return final_state


def scan_outputs(state_in, step_size, x_float, decay_rate, b_rows, c_rows, skip_gain):

    def scan_advance(state, inputs):
        step_now, x_now, b_now, c_now = inputs
        state = (
            jnp.exp(-step_now[None, :] * decay_rate) * state
            + (step_now * x_now)[None, :] * b_now[:, None]
        )
        y_now = jnp.sum(c_now[:, None] * state, axis=0) + skip_gain * x_now
        return (state, y_now)

    _, outputs = lax.scan(scan_advance, state_in, (step_size, x_float, b_rows, c_rows), unroll=8)
    return outputs


def on_device(
    x_in,
    z_in,
    step_raw,
    step_bias,
    decay_rate,
    b_coef,
    c_coef,
    skip_gain,
    out_proj,
    residual,
    norm_gain,
    router_weight,
    expert_ids,
    gate_weight,
    up_weight,
    down_weight,
):
    step_size = jax.nn.softplus(step_raw.astype(jnp.float32) + step_bias[None, :])
    x_float = x_in.astype(jnp.float32)
    b_rows = b_coef.astype(jnp.float32).T
    c_rows = c_coef.astype(jnp.float32).T
    state_end = end_state(step_size, x_float, decay_rate, b_rows)
    decay_end = jnp.exp(-decay_rate * jnp.sum(step_size, axis=0)[None, :])
    identity = (jnp.ones_like(decay_end), jnp.zeros_like(state_end))
    carried = entering((decay_end, state_end), "seq", pair_combine, identity)
    state_in = carried[1]
    scanned = scan_outputs(state_in, step_size, x_float, decay_rate, b_rows, c_rows, skip_gain)
    gated = (scanned * jax.nn.silu(z_in.astype(jnp.float32))).astype(jnp.bfloat16)
    column_part = jnp.dot(
        lax.all_gather(gated, "seq", axis=0, tiled=True),
        out_proj,
        preferred_element_type=jnp.float32,
    )
    seq_count = lax.axis_size("seq")
    expert_count = lax.axis_size("expert")
    rows = residual.shape[0]
    grouped = column_part.reshape(seq_count, expert_count, rows, column_part.shape[1])
    summed = lax.psum_scatter(grouped, "expert", scatter_dimension=1, tiled=True)
    arranged = jnp.transpose(summed[:, 0], (1, 0, 2))
    swapped = lax.all_to_all(arranged, "seq", split_axis=1, concat_axis=1, tiled=True)
    mamba_out = swapped.reshape(rows, -1)
    hidden = (residual.astype(jnp.float32) + mamba_out).astype(jnp.bfloat16)
    hidden_f = hidden.astype(jnp.float32)
    width_d = hidden.shape[1]
    scale_cols = width_d // BLOCK
    normed = (
        hidden_f
        * lax.rsqrt(jnp.mean(hidden_f * hidden_f, axis=-1, keepdims=True) + 1e-05)
        * norm_gain[None, :]
    )
    blocked = normed.reshape(rows, scale_cols, BLOCK)
    scales = (jnp.max(jnp.abs(blocked), axis=-1) / 448.0 + 1e-06).astype(jnp.bfloat16)
    quant = (blocked / scales.astype(jnp.float32)[..., None]).astype(jnp.bfloat16)
    restored = (
        (quant.astype(jnp.float32) * scales.astype(jnp.float32)[..., None])
        .astype(jnp.bfloat16)
        .reshape(rows, width_d)
    )
    experts = router_weight.shape[1]
    probs = jax.nn.sigmoid(jnp.dot(restored, router_weight, preferred_element_type=jnp.float32))
    picks = expert_ids[:, :, None] == jnp.arange(experts, dtype=jnp.int32)[None, None, :]
    chosen = jnp.sum(jnp.where(picks, probs[:, None, :], jnp.float32(0.0)), axis=-1)
    weights = chosen / jnp.sum(chosen, axis=-1, keepdims=True)
    coef = jnp.sum(jnp.where(expert_ids == 0, weights, jnp.float32(0.0)), axis=1)
    wanted = jnp.any(expert_ids == 0, axis=1)
    wanted_int = wanted.astype(jnp.int32)
    slot_pos = jnp.cumsum(wanted_int) - wanted_int
    capacity = rows // 2
    table = (
        (slot_pos[None, :] == jnp.arange(capacity, dtype=jnp.int32)[:, None]) & wanted[None, :]
    ).astype(jnp.bfloat16)
    send_quant = jnp.dot(
        table, quant.reshape(rows, width_d), preferred_element_type=jnp.float32
    ).astype(jnp.bfloat16)
    send_scale = jnp.dot(table, scales, preferred_element_type=jnp.float32).astype(jnp.bfloat16)
    all_quant, all_scale = (
        lax.all_gather(send_quant, ("seq", "expert"), axis=0, tiled=True),
        lax.all_gather(send_scale, ("seq", "expert"), axis=0, tiled=True),
    )
    slots = all_quant.shape[0]
    inputs = (
        (
            all_quant.reshape(slots, scale_cols, BLOCK).astype(jnp.float32)
            * all_scale.astype(jnp.float32)[..., None]
        )
        .astype(jnp.bfloat16)
        .reshape(slots, width_d)
    )
    gate_value = jnp.dot(inputs, gate_weight, preferred_element_type=jnp.float32)
    up_value = jnp.dot(inputs, up_weight, preferred_element_type=jnp.float32)
    active = (jax.nn.silu(gate_value) * up_value).astype(jnp.bfloat16)
    own_sum = lax.psum_scatter(
        jnp.dot(active, down_weight, preferred_element_type=jnp.float32).astype(jnp.bfloat16),
        ("seq", "expert"),
        scatter_dimension=0,
        tiled=True,
    )
    returned = jnp.dot(table.T, own_sum, preferred_element_type=jnp.float32)
    return (hidden_f + coef[:, None] * returned).astype(jnp.bfloat16)


def solution(mesh):
    return jax.shard_map(
        on_device,
        mesh=mesh,
        in_specs=(
            P(("dp", "seq"), "expert"),
            P(("dp", "seq"), "expert"),
            P(("dp", "seq"), "expert"),
            P("expert"),
            P(None, "expert"),
            P(None, ("dp", "seq")),
            P(None, ("dp", "seq")),
            P("expert"),
            P("expert", "seq"),
            P(("dp", "seq", "expert"), None),
            P(),
            P(),
            P(("dp", "seq", "expert"), None),
            P(None, ("seq", "expert")),
            P(None, ("seq", "expert")),
            P(("seq", "expert"), None),
        ),
        out_specs=P(("dp", "seq", "expert"), None),
        check_vma=False,
    )
```

profile of v0, /device:TPU:0, one launch (start us, length us, event | category | flops | bytes accessed | tf_op | source)
XLA Modules:
  0.0 533.8 jit_solution(4677953557653513335)
XLA Ops:
  7.4 1.1 bitcast_convert_fusion
  8.5 1.7 fusion.67
  10.2 21.8 %while.38 = (s32[]{:T(128)}, f32[16,2048]{1,0:T(8,128)S(1)}, f32[16,8,2048]{2,1,0:T(8,128)S(1)}, f32[16,2048]{1,0:T(8,128)}, f32[16,8,2048]{2,1,0:T(8,128)S(1)},...) while((s32[]{:T(128)}, f32[16,2048]{1,0:T(8,128)S(1)}, ...), condition=%wide.region_2.3_spmd.clone, body=%wide.region_1.2_spmd.clone.sunk | while | flops 1114122 | bytes 789271 | solution.py:38
  10.4 1.2 fusion.106
  11.8 1.2 fusion.106
  13.2 1.2 fusion.106
  14.5 1.2 fusion.106
  15.9 1.2 fusion.106
  17.2 1.2 fusion.106
  18.6 1.2 fusion.106
  20.0 1.2 fusion.106
  21.3 1.2 fusion.106
  22.7 1.2 fusion.106
  24.1 1.2 fusion.106
  25.4 1.2 fusion.106
  26.8 1.2 fusion.106
  28.2 1.2 fusion.106
  29.5 1.2 fusion.106
  30.9 1.2 fusion.106
  32.8 1.6 multiply_exponential_fusion
  34.6 24.2 %all-gather.13.cloned.1.call-done = f32[128,2048]{1,0:T(8,128)} async-done(((f32[16,2048]{1,0:T(8,128)}), f32[128,2048]{1,0:T(8,128)}) %all-gather.13.cloned.1.call-update) | async-done | bytes 1048592 | tf_op jit(solution)/shard_map/all_gather | solution.py:11
  58.8 25.1 %all-gather.11.cloned.1.call-done = f32[128,2048]{1,0:T(8,128)} async-done(((f32[16,2048]{1,0:T(8,128)}), f32[128,2048]{1,0:T(8,128)}) %all-gather.11.cloned.1.call-update) | async-done | bytes 1048592 | tf_op jit(solution)/shard_map/all_gather | solution.py:11
  84.0 7.6 %while.39 = (s32[]{:T(128)}, f32[16,2048]{1,0:T(8,128)S(1)}, s32[]{:T(128)}, f32[8,16,2048]{2,1,0:T(8,128)}, f32[8,16,2048]{2,1,0:T(8,128)}, /*index=5*/s32[]{:T(128)}, s32[]{:T(128)}) while((s32[]{:T(128)}, f32[16,2048]{1,0:T(8,128)S(1)}, s32[]{:T(128)}, f32[8,16,2048]{2,1,0:T(8,128)}, f32[8,16,2048]{2,1,0:T(8,128)}, ...), condition=%wide.region_4.5_spmd.clone, body=%wide.region_3.4_spmd.clone.sunk | while | flops 131076 | bytes 524397 | solution.py:20
  91.6 71.2 %while.37 = (s32[]{:T(128)}, f32[16,2048]{1,0:T(8,128)S(1)}, f32[16,8,2048]{2,1,0:T(8,128)}, f32[16,8,2048]{2,1,0:T(8,128)S(1)}, f32[16,2048]{1,0:T(8,128)}, /*i...) while((s32[]{:T(128)}, f32[16,2048]{1,0:T(8,128)S(1)}, ...), condition=%wide.region_14.15_spmd, body=%wide.region_5.14_spmd.sunk | while | flops 2408457 | bytes 2078409 | solution.py:53
  92.9 1.2 multiply_reduce_fusion.11
  94.1 1.1 multiply_reduce_fusion.12
  97.3 1.2 multiply_reduce_fusion.11
  98.5 1.1 multiply_reduce_fusion.12
  101.8 1.2 multiply_reduce_fusion.11
  106.2 1.2 multiply_reduce_fusion.11
  107.4 1.1 multiply_reduce_fusion.12
  110.7 1.2 multiply_reduce_fusion.11
  111.9 1.1 multiply_reduce_fusion.12
  115.1 1.2 multiply_reduce_fusion.11
  119.6 1.2 multiply_reduce_fusion.11
  120.8 1.1 multiply_reduce_fusion.12
  124.0 1.2 multiply_reduce_fusion.11
  125.2 1.1 multiply_reduce_fusion.12
  128.5 1.2 multiply_reduce_fusion.11
  129.7 1.1 multiply_reduce_fusion.12
  132.9 1.2 multiply_reduce_fusion.11
  134.1 1.1 multiply_reduce_fusion.12
  137.4 1.2 multiply_reduce_fusion.11
  138.6 1.1 multiply_reduce_fusion.12
  141.8 1.2 multiply_reduce_fusion.11
  143.0 1.1 multiply_reduce_fusion.12
  146.3 1.2 multiply_reduce_fusion.11
  150.7 1.2 multiply_reduce_fusion.11
  155.1 1.2 multiply_reduce_fusion.11
  159.6 1.2 multiply_reduce_fusion.11
  162.8 2.3 fusion.66
  165.2 32.3 %all-gather.7.cloned.1.call-done = bf16[1024,2048]{1,0:T(8,128)(2,1)} async-done(((bf16[128,2048]{1,0:T(8,128)(2,1)}), bf16[1024,2048]{1,0:T(8,128)(2,1)}) %all-gather.7.cloned.1.call-update) | async-done | bytes 4194320 | tf_op jit(solution)/shard_map/all_gather | solution.py:87
  197.5 9.9 %fusion.91 = f32[1024,1024]{1,0:T(8,128)} fusion(bf16[1024,2048]{1,0:T(8,128)(2,1)} %all-gather.7.cloned.1.call-done, bf16[2048,1024]{1,0:T(8,128)(2,1)} %param.30), kind=kOutput, calls=%fused_computation.200 | convolution fusion | flops 4294967296 | bytes 12582912 | tf_op jit(solution)/shard_map/dot_general | solution.py:86
  208.0 92.1 %all-reduce.3.cloned.1.call-done = f32[8,4,32,1024]{3,2,1,0:T(8,128)} async-done(((f32[8,4,32,1024]{3,2,1,0:T(8,128)}), f32[8,4,32,1024]{3,2,1,0:T(8,128)}) %all-reduce.3.cloned.1.call-update) | async-done | bytes 4194320
  300.2 3.0 dynamic-slice_bitcast_fusion
  303.1 4.4 all-to-all-start
  307.9 15.6 %all-to-all-done = f32[32,8,1024]{2,0,1:T(8,128)S(1)} async-done(((f32[32,8,1024]{2,0,1:T(8,128)}), f32[32,8,1024]{2,0,1:T(8,128)S(1)}, u32[]{:S(2)}, u32[]{:S(2)}) %all-to-all-start) | async-done | bytes 1048608 | tf_op jit(solution)/shard_map/all_to_all | solution.py:97
  326.7 38.1 %all_gather.27 = bf16[512,64]{1,0:T(8,128)(2,1)S(1)} all-gather(bf16[16,64]{1,0:T(8,128)(2,1)S(1)} %convolution_convert_fusion.2), channel_id=1, replica_groups=mesh['dp'=4,'seq'=8,'expert'=4] {'seq','expert'}, dimensions={0}, use_global_device_ids=true | all-gather | bytes 67584 | tf_op jit(solution)/shard_map/all_gather | solution.py:135
  364.9 12.8 %all-gather.9.cloned.1.call-done = bf16[512,8192]{1,0:T(8,128)(2,1)} async-done(((bf16[16,8192]{1,0:T(8,128)(2,1)}), bf16[512,8192]{1,0:T(8,128)(2,1)}) %all-gather.9.cloned.1.call-update) | async-done | bytes 8388624 | tf_op jit(solution)/shard_map/all_gather | solution.py:134
  377.7 8.0 %mul.821 = f32[512,64,128]{2,1,0:T(8,128)} broadcast(bf16[512,64]{1,0:T(8,128)(2,1)S(1)} %all_gather.27), dimensions={0,1} | broadcast | bytes 16842752 | tf_op jit(solution)/shard_map/mul | solution.py:140
  385.6 18.4 %fusion.89 = f32[512,384]{1,0:T(8,128)S(1)} fusion(bf16[8192,384]{1,0:T(8,128)(2,1)} %param.35, f32[64,8,64,128]{3,2,1,0:T(8,128)} %bitcast.286, bf16[512,8192]{1,0:T(8,128)(2,1)S(1)} %copy-done.1), kind=kOutput, calls=%fused_computation.199 | convolution fusion | flops 3233808384 | bytes 32243712 | tf_op jit(solution)/shard_map/dot_general | solution.py:146
  404.0 28.3 %convolution_convert_fusion = bf16[512,8192]{1,0:T(8,128)(2,1)} fusion(bf16[384,8192]{1,0:T(8,128)(2,1)} %param.37, bf16[8192,384]{1,0:T(8,128)(2,1)} %param.36, f32[512,384]{1,0:T(8,128)S(1)} %fusion.89, f32[64,8,64,128]{3,2,1,0:T(8,128)} %bitcast.287, bf16[512,8192]{1,0:T(8,128)(2,1)} %all-gather.9.cloned.1.call-done), kind=kOutput, calls=%fused_computation.137 | convolution fusion | flops 6460407808 | bytes 46923776 | tf_op jit(solution)/shard_map/dot_general | solution.py:150
  433.2 91.7 %reduce-scatter.5.cloned.1.call-done = bf16[16,8192]{1,0:T(8,128)(2,1)} async-done(((bf16[512,8192]{1,0:T(8,128)(2,1)}), bf16[16,8192]{1,0:T(8,128)(2,1)}) %reduce-scatter.5.cloned.1.call-update) | async-done | bytes 262160 | tf_op jit(solution)/shard_map/reduce_scatter | solution.py:149
  524.9 2.1 fusion.50
  (249 shorter events, 56.6 us)
Async XLA Ops:
  6.5 425.8 %copy-start = (bf16[8192,16]{0,1:T(8,128)(2,1)S(1)}, bf16[8192,16]{0,1:T(8,128)(2,1)}, u32[]{:S(2)}) copy-start(bf16[8192,16]{0,1:T(8,128)(2,1)} %param.33) | copy-start | bytes 786436
  6.5 27.9 %copy-start.7 = (bf16[16,128]{1,0:T(8,128)(2,1)S(1)}, bf16[16,128]{1,0:T(8,128)(2,1)}, u32[]{:S(2)}) copy-start(bf16[16,128]{1,0:T(8,128)(2,1)} %param.28) | copy-start | bytes 12292
  6.5 85.0 %copy-start.5 = (f32[2048]{0:T(1024)S(1)}, f32[2048]{0:T(1024)}, u32[]{:S(2)}) copy-start(f32[2048]{0:T(1024)} %param.29) | copy-start | bytes 24580
  6.5 52.3 %all-gather.13.cloned.1.call-start = ((), (), s32[]{:S(2)}) async-start(), calls=%async_computation.6 | async-start | bytes 1179648 | tf_op jit(solution)/shard_map/all_gather | solution.py:11
  32.1 0.6 copy-start.2
  32.1 130.7 %copy-start.4 = (bf16[128,2048]{1,0:T(8,128)(2,1)S(1)}, bf16[128,2048]{1,0:T(8,128)(2,1)}, u32[]{:S(2)}) copy-start(bf16[128,2048]{1,0:T(8,128)(2,1)} %param.23) | copy-start | bytes 1572868
  32.7 51.2 %all-gather.11.cloned.1.call-start = ((), (), s32[]{:S(2)}) async-start(), calls=%async_computation.5 | async-start | bytes 1179648 | tf_op jit(solution)/shard_map/all_gather | solution.py:11
  34.4 163.1 %all-gather.7.cloned.1.call-start = ((), (), s32[]{:S(2)}) async-start(), calls=%async_computation.2 | async-start | bytes 4718592 | tf_op jit(solution)/shard_map/all_gather | solution.py:87
  165.1 42.3 %copy-start.9 = (u32[128]{0:T(128)S(1)}, u32[128]{0:T(128)}, u32[]{:S(2)}) copy-start(u32[128]{0:T(128)} %constant.87) | copy-start | bytes 1540
  165.2 135.0 %all-reduce.3.cloned.1.call-start = ((), (), s32[]{:S(2)}) async-start(), calls=%async_computation.7 | async-start | bytes 8388608
  207.4 100.2 %copy-start.8 = (s32[32,2]{0,1:T(2,128)S(1)}, s32[32,2]{0,1:T(2,128)}, u32[]{:S(2)}) copy-start(s32[32,2]{0,1:T(2,128)} %param.34) | copy-start | bytes 772
  207.4 116.2 %copy-start.3 = (bf16[32,8192]{1,0:T(8,128)(2,1)S(1)}, bf16[32,8192]{1,0:T(8,128)(2,1)}, u32[]{:S(2)}) copy-start(bf16[32,8192]{1,0:T(8,128)(2,1)} %param.31) | copy-start | bytes 1572868
  207.4 116.5 %copy-start.6 = (f32[8192]{0:T(1024)S(1)}, f32[8192]{0:T(1024)}, u32[]{:S(2)}) copy-start(f32[8192]{0:T(1024)} %param.32) | copy-start | bytes 98308
  303.1 20.4 %all-to-all-start = ((f32[32,8,1024]{2,0,1:T(8,128)}), f32[32,8,1024]{2,0,1:T(8,128)S(1)}, u32[]{:S(2)}, u32[]{:S(2)}) async-start(f32[32,8,1024]{2,0,1:T(8,128)} %dynamic-slice_bitcast_fusion), calls=%async_computation | async-start | bytes 2097152 | tf_op jit(solution)/shard_map/all_to_all | solution.py:97
  307.5 70.1 %all-gather.9.cloned.1.call-start = ((), (), s32[]{:S(2)}) async-start(), calls=%async_computation.3 | async-start | bytes 8650752 | tf_op jit(solution)/shard_map/all_gather | solution.py:134
  326.6 198.3 %reduce-scatter.5.cloned.1.call-start = ((), (), s32[]{:S(2)}) async-start(), calls=%async_computation.4 | async-start | bytes 8650752 | tf_op jit(solution)/shard_map/reduce_scatter | solution.py:149
  377.7 8.0 %copy-start.1 = (bf16[512,8192]{1,0:T(8,128)(2,1)S(1)}, bf16[512,8192]{1,0:T(8,128)(2,1)}, u32[]{:S(2)}) copy-start(bf16[512,8192]{1,0:T(8,128)(2,1)} %all-gather.9.cloned.1.call-done) | copy-start | bytes 25165828
Sparse Core Ops, SparseCore 0:
  32.9 25.9 all-gather.12
  60.5 23.3 all-gather.10
  165.3 32.1 all-gather.6
  207.6 92.5 all-reduce.2
  326.7 50.9 all-gather.8
  432.5 92.3 reduce-scatter.4
where the time goes:
time: 535 us; the launch traced here: 534 us
  waiting for transfers between devices  294 us (55%)
  other arithmetic  96.1 us (18%)
  matrix products  60.5 us (11%)
  blocking collectives  38.1 us (7%)
  local copies, waits for them, and re-layouts  25.5 us (5%)
  between operations  13.7 us (3%)
    unnamed x7, waiting for transfers between devices  92.2 us
    reduce_scatter x1, waiting for transfers between devices, on_device(): lax.psum_scatter(jnp.dot(active, down_weight, preferred_element_type=jnp....  91.7 us
    reduce_sum x48, other arithmetic, scan_advance(): y_now = jnp.sum(c_now[:, None] * state, axis=0) + skip_gain * x_now  54.8 us
    all_gather x2, waiting for transfers between devices, entering(): pieces = jax.tree.map(lambda part: lax.all_gather(part, axis), value)  49.4 us
    all_gather x1, blocking collectives, on_device(): lax.all_gather(send_scale, ('seq', 'expert'), axis=0, tiled=True)  38.1 us
    all_gather x1, waiting for transfers between devices, on_device(): lax.all_gather(gated, 'seq', axis=0, tiled=True)  32.3 us
    dot_general x1, matrix products, on_device(): jnp.dot(active, down_weight, preferred_element_type=jnp.float32)  28.3 us
    add x16, other arithmetic, end_advance(): jnp.exp(-step_now[None, :] * decay_rate) * state  18.7 us
  transfers between devices with their start and end apart: 7, of which 7 were waited for; matrix products, arithmetic and copies ran while one was open for 1% of the time, Pallas kernels for 0%

commit v1 on v0

--- a/solution.py
+++ b/solution.py
@@ -94,7 +94,10 @@
     grouped = column_part.reshape(seq_count, expert_count, rows, column_part.shape[1])
     summed = lax.psum_scatter(grouped, "expert", scatter_dimension=1, tiled=True)
     arranged = jnp.transpose(summed[:, 0], (1, 0, 2))
-    swapped = lax.all_to_all(arranged, "seq", split_axis=1, concat_axis=1, tiled=True)
+    swapped = jnp.concatenate(
+        lax.all_to_all(jnp.stack(jnp.split(arranged, lax.axis_size("seq"), axis=1)), "seq", 0, 0),
+        axis=1,
+    )
     mamba_out = swapped.reshape(rows, -1)
     hidden = (residual.astype(jnp.float32) + mamba_out).astype(jnp.bfloat16)
     hidden_f = hidden.astype(jnp.float32)

time: 535 us -> 540 us (level)
  no operation moved by 1% of the time
where the time goes in v1:
time: 540 us; the launch traced here: 538 us
  waiting for transfers between devices  294 us (54%)
  other arithmetic  96.2 us (18%)
  matrix products  60.4 us (11%)
  blocking collectives  38.1 us (7%)
  local copies, waits for them, and re-layouts  29.8 us (6%)
  between operations  13.7 us (3%)
    unnamed x7, waiting for transfers between devices  92.2 us
    reduce_scatter x1, waiting for transfers between devices, on_device(): lax.psum_scatter(jnp.dot(active, down_weight, preferred_element_type=jnp....  91.7 us
    reduce_sum x48, other arithmetic, scan_advance(): y_now = jnp.sum(c_now[:, None] * state, axis=0) + skip_gain * x_now  54.9 us
    all_gather x2, waiting for transfers between devices, entering(): pieces = jax.tree.map(lambda part: lax.all_gather(part, axis), value)  49.4 us
    all_gather x1, blocking collectives, on_device(): lax.all_gather(send_scale, ('seq', 'expert'), axis=0, tiled=True)  38.1 us
    all_gather x1, waiting for transfers between devices, on_device(): lax.all_gather(gated, 'seq', axis=0, tiled=True)  32.3 us
    dot_general x1, matrix products, on_device(): jnp.dot(active, down_weight, preferred_element_type=jnp.float32)  28.3 us
    add x16, other arithmetic, end_advance(): jnp.exp(-step_now[None, :] * decay_rate) * state  18.5 us
  transfers between devices with their start and end apart: 7, of which 7 were waited for; matrix products, arithmetic and copies ran while one was open for 1% of the time, Pallas kernels for 0%

profile of v1, /device:TPU:0, one launch (start us, length us, event | category | flops | bytes accessed | tf_op | source)
XLA Modules:
  0.0 538.1 jit_solution(14334320308884802448)
XLA Ops:
  7.4 1.1 bitcast_convert_fusion
  8.5 1.7 fusion.67
  10.2 21.7 %while.38 = (s32[]{:T(128)}, f32[16,2048]{1,0:T(8,128)S(1)}, f32[16,8,2048]{2,1,0:T(8,128)S(1)}, f32[16,2048]{1,0:T(8,128)}, f32[16,8,2048]{2,1,0:T(8,128)S(1)},...) while((s32[]{:T(128)}, f32[16,2048]{1,0:T(8,128)S(1)}, ...), condition=%wide.region_2.3_spmd.clone, body=%wide.region_1.2_spmd.clone.sunk | while | flops 1114122 | bytes 789271 | solution.py:38
  10.4 1.2 fusion.114
  11.8 1.2 fusion.114
  13.1 1.2 fusion.114
  14.5 1.2 fusion.114
  15.8 1.2 fusion.114
  17.2 1.2 fusion.114
  18.6 1.2 fusion.114
  19.9 1.2 fusion.114
  21.3 1.2 fusion.114
  22.6 1.2 fusion.114
  24.0 1.2 fusion.114
  25.3 1.2 fusion.114
  26.7 1.2 fusion.114
  28.0 1.2 fusion.114
  29.4 1.2 fusion.114
  30.7 1.2 fusion.114
  32.6 1.6 multiply_exponential_fusion
  34.5 24.2 %all-gather.13.cloned.1.call-done = f32[128,2048]{1,0:T(8,128)} async-done(((f32[16,2048]{1,0:T(8,128)}), f32[128,2048]{1,0:T(8,128)}) %all-gather.13.cloned.1.call-update) | async-done | bytes 1048592 | tf_op jit(solution)/shard_map/all_gather | solution.py:11
  58.7 25.1 %all-gather.11.cloned.1.call-done = f32[128,2048]{1,0:T(8,128)} async-done(((f32[16,2048]{1,0:T(8,128)}), f32[128,2048]{1,0:T(8,128)}) %all-gather.11.cloned.1.call-update) | async-done | bytes 1048592 | tf_op jit(solution)/shard_map/all_gather | solution.py:11
  83.8 7.6 %while.39 = (s32[]{:T(128)}, f32[16,2048]{1,0:T(8,128)S(1)}, s32[]{:T(128)}, f32[8,16,2048]{2,1,0:T(8,128)}, f32[8,16,2048]{2,1,0:T(8,128)}, /*index=5*/s32[]{:T(128)}, s32[]{:T(128)}) while((s32[]{:T(128)}, f32[16,2048]{1,0:T(8,128)S(1)}, s32[]{:T(128)}, f32[8,16,2048]{2,1,0:T(8,128)}, f32[8,16,2048]{2,1,0:T(8,128)}, ...), condition=%wide.region_4.5_spmd.clone, body=%wide.region_3.4_spmd.clone.sunk | while | flops 131076 | bytes 524397 | solution.py:20
  91.5 71.4 %while.37 = (s32[]{:T(128)}, f32[16,2048]{1,0:T(8,128)S(1)}, f32[16,8,2048]{2,1,0:T(8,128)}, f32[16,8,2048]{2,1,0:T(8,128)S(1)}, f32[16,2048]{1,0:T(8,128)}, /*i...) while((s32[]{:T(128)}, f32[16,2048]{1,0:T(8,128)S(1)}, ...), condition=%wide.region_14.15_spmd, body=%wide.region_5.14_spmd.sunk | while | flops 2408457 | bytes 2078409 | solution.py:53
  92.7 1.2 multiply_reduce_fusion.11
  94.0 1.1 multiply_reduce_fusion.12
  97.2 1.2 multiply_reduce_fusion.11
  101.7 1.2 multiply_reduce_fusion.11
  102.9 1.1 multiply_reduce_fusion.12
  106.1 1.2 multiply_reduce_fusion.11
  107.3 1.1 multiply_reduce_fusion.12
  110.6 1.2 multiply_reduce_fusion.11
  115.0 1.2 multiply_reduce_fusion.11
  116.3 1.1 multiply_reduce_fusion.12
  119.5 1.2 multiply_reduce_fusion.11
  124.0 1.2 multiply_reduce_fusion.11
  125.2 1.1 multiply_reduce_fusion.12
  128.4 1.2 multiply_reduce_fusion.11
  129.6 1.1 multiply_reduce_fusion.12
  132.9 1.2 multiply_reduce_fusion.11
  134.1 1.1 multiply_reduce_fusion.12
  137.3 1.2 multiply_reduce_fusion.11
  138.6 1.1 multiply_reduce_fusion.12
  141.8 1.2 multiply_reduce_fusion.11
  146.3 1.2 multiply_reduce_fusion.11
  150.7 1.2 multiply_reduce_fusion.11
  155.2 1.2 multiply_reduce_fusion.11
  156.4 1.1 multiply_reduce_fusion.12
  159.6 1.2 multiply_reduce_fusion.11
  160.9 1.1 multiply_reduce_fusion.12
  162.9 2.3 fusion.66
  165.3 32.3 %all-gather.7.cloned.1.call-done = bf16[1024,2048]{1,0:T(8,128)(2,1)} async-done(((bf16[128,2048]{1,0:T(8,128)(2,1)}), bf16[1024,2048]{1,0:T(8,128)(2,1)}) %all-gather.7.cloned.1.call-update) | async-done | bytes 4194320 | tf_op jit(solution)/shard_map/all_gather | solution.py:87
  197.5 9.9 %fusion.99 = f32[1024,1024]{1,0:T(8,128)} fusion(bf16[1024,2048]{1,0:T(8,128)(2,1)} %all-gather.7.cloned.1.call-done, bf16[2048,1024]{1,0:T(8,128)(2,1)} %param.30), kind=kOutput, calls=%fused_computation.216 | convolution fusion | flops 4294967296 | bytes 12582912 | tf_op jit(solution)/shard_map/dot_general | solution.py:86
  208.0 92.1 %all-reduce.3.cloned.1.call-done = f32[8,4,32,1024]{3,2,1,0:T(8,128)} async-done(((f32[8,4,32,1024]{3,2,1,0:T(8,128)}), f32[8,4,32,1024]{3,2,1,0:T(8,128)}) %all-reduce.3.cloned.1.call-update) | async-done | bytes 4194320
  300.2 2.0 dynamic-slice_bitcast_fusion
  307.4 4.4 all-to-all-start
  312.2 15.6 %all-to-all-done = f32[8,32,1,1024]{3,1,2,0:T(8,128)S(1)} async-done(((f32[8,32,1,1024]{3,1,2,0:T(8,128)}), f32[8,32,1,1024]{3,1,2,0:T(8,128)S(1)}, u32[]{:S(2)}, u32[]{:S(2)}) %all-to-all-start) | async-done | bytes 1048608 | tf_op jit(solution)/shard_map/all_to_all | solution.py:98
  331.0 38.1 %all_gather.27 = bf16[512,64]{1,0:T(8,128)(2,1)S(1)} all-gather(bf16[16,64]{1,0:T(8,128)(2,1)S(1)} %convolution_convert_fusion.2), channel_id=1, replica_groups=mesh['dp'=4,'seq'=8,'expert'=4] {'seq','expert'}, dimensions={0}, use_global_device_ids=true | all-gather | bytes 67584 | tf_op jit(solution)/shard_map/all_gather | solution.py:138
  369.2 12.8 %all-gather.9.cloned.1.call-done = bf16[512,8192]{1,0:T(8,128)(2,1)} async-done(((bf16[16,8192]{1,0:T(8,128)(2,1)}), bf16[512,8192]{1,0:T(8,128)(2,1)}) %all-gather.9.cloned.1.call-update) | async-done | bytes 8388624 | tf_op jit(solution)/shard_map/all_gather | solution.py:137
  382.0 8.0 %mul.821 = f32[512,64,128]{2,1,0:T(8,128)} broadcast(bf16[512,64]{1,0:T(8,128)(2,1)S(1)} %all_gather.27), dimensions={0,1} | broadcast | bytes 16842752 | tf_op jit(solution)/shard_map/mul | solution.py:143
  389.9 18.4 %fusion.97 = f32[512,384]{1,0:T(8,128)S(1)} fusion(bf16[8192,384]{1,0:T(8,128)(2,1)} %param.35, f32[64,8,64,128]{3,2,1,0:T(8,128)} %bitcast.323, bf16[512,8192]{1,0:T(8,128)(2,1)S(1)} %copy-done.1), kind=kOutput, calls=%fused_computation.215 | convolution fusion | flops 3233808384 | bytes 32243712 | tf_op jit(solution)/shard_map/dot_general | solution.py:149
  408.3 28.3 %convolution_convert_fusion = bf16[512,8192]{1,0:T(8,128)(2,1)} fusion(bf16[384,8192]{1,0:T(8,128)(2,1)} %param.37, bf16[8192,384]{1,0:T(8,128)(2,1)} %param.36, f32[512,384]{1,0:T(8,128)S(1)} %fusion.97, f32[64,8,64,128]{3,2,1,0:T(8,128)} %bitcast.324, bf16[512,8192]{1,0:T(8,128)(2,1)} %all-gather.9.cloned.1.call-done), kind=kOutput, calls=%fused_computation.137 | convolution fusion | flops 6460407808 | bytes 46923776 | tf_op jit(solution)/shard_map/dot_general | solution.py:153
  437.5 91.7 %reduce-scatter.5.cloned.1.call-done = bf16[16,8192]{1,0:T(8,128)(2,1)} async-done(((bf16[512,8192]{1,0:T(8,128)(2,1)}), bf16[16,8192]{1,0:T(8,128)(2,1)}) %reduce-scatter.5.cloned.1.call-update) | async-done | bytes 262160 | tf_op jit(solution)/shard_map/reduce_scatter | solution.py:152
  529.2 2.1 fusion.50
  (257 shorter events, 62.0 us)
Async XLA Ops:
  6.5 430.1 %copy-start = (bf16[8192,16]{0,1:T(8,128)(2,1)S(1)}, bf16[8192,16]{0,1:T(8,128)(2,1)}, u32[]{:S(2)}) copy-start(bf16[8192,16]{0,1:T(8,128)(2,1)} %param.33) | copy-start | bytes 786436
  6.5 27.8 %copy-start.7 = (bf16[16,128]{1,0:T(8,128)(2,1)S(1)}, bf16[16,128]{1,0:T(8,128)(2,1)}, u32[]{:S(2)}) copy-start(bf16[16,128]{1,0:T(8,128)(2,1)} %param.28) | copy-start | bytes 12292
  6.5 84.9 %copy-start.5 = (f32[2048]{0:T(1024)S(1)}, f32[2048]{0:T(1024)}, u32[]{:S(2)}) copy-start(f32[2048]{0:T(1024)} %param.29) | copy-start | bytes 24580
  6.5 52.2 %all-gather.13.cloned.1.call-start = ((), (), s32[]{:S(2)}) async-start(), calls=%async_computation.6 | async-start | bytes 1179648 | tf_op jit(solution)/shard_map/all_gather | solution.py:11
  31.9 0.6 copy-start.2
  31.9 130.9 %copy-start.4 = (bf16[128,2048]{1,0:T(8,128)(2,1)S(1)}, bf16[128,2048]{1,0:T(8,128)(2,1)}, u32[]{:S(2)}) copy-start(bf16[128,2048]{1,0:T(8,128)(2,1)} %param.23) | copy-start | bytes 1572868
  32.6 51.2 %all-gather.11.cloned.1.call-start = ((), (), s32[]{:S(2)}) async-start(), calls=%async_computation.5 | async-start | bytes 1179648 | tf_op jit(solution)/shard_map/all_gather | solution.py:11
  34.3 163.3 %all-gather.7.cloned.1.call-start = ((), (), s32[]{:S(2)}) async-start(), calls=%async_computation.2 | async-start | bytes 4718592 | tf_op jit(solution)/shard_map/all_gather | solution.py:87
  165.2 42.3 %copy-start.9 = (u32[128]{0:T(128)S(1)}, u32[128]{0:T(128)}, u32[]{:S(2)}) copy-start(u32[128]{0:T(128)} %constant.87) | copy-start | bytes 1540
  165.2 134.9 %all-reduce.3.cloned.1.call-start = ((), (), s32[]{:S(2)}) async-start(), calls=%async_computation.7 | async-start | bytes 8388608
  207.4 104.5 %copy-start.8 = (s32[32,2]{0,1:T(2,128)S(1)}, s32[32,2]{0,1:T(2,128)}, u32[]{:S(2)}) copy-start(s32[32,2]{0,1:T(2,128)} %param.34) | copy-start | bytes 772
  207.4 120.5 %copy-start.3 = (bf16[32,8192]{1,0:T(8,128)(2,1)S(1)}, bf16[32,8192]{1,0:T(8,128)(2,1)}, u32[]{:S(2)}) copy-start(bf16[32,8192]{1,0:T(8,128)(2,1)} %param.31) | copy-start | bytes 1572868
  207.4 120.8 %copy-start.6 = (f32[8192]{0:T(1024)S(1)}, f32[8192]{0:T(1024)}, u32[]{:S(2)}) copy-start(f32[8192]{0:T(1024)} %param.32) | copy-start | bytes 98308
  307.4 20.4 %all-to-all-start = ((f32[8,32,1,1024]{3,1,2,0:T(8,128)}), f32[8,32,1,1024]{3,1,2,0:T(8,128)S(1)}, u32[]{:S(2)}, u32[]{:S(2)}) async-start(f32[8,32,1,1024]{3,1,2,0:T(8,128)} %fusion.71), calls=%async_computation | async-start | bytes 2097152 | tf_op jit(solution)/shard_map/all_to_all | solution.py:98
  311.8 70.1 %all-gather.9.cloned.1.call-start = ((), (), s32[]{:S(2)}) async-start(), calls=%async_computation.3 | async-start | bytes 8650752 | tf_op jit(solution)/shard_map/all_gather | solution.py:137
  330.9 198.3 %reduce-scatter.5.cloned.1.call-start = ((), (), s32[]{:S(2)}) async-start(), calls=%async_computation.4 | async-start | bytes 8650752 | tf_op jit(solution)/shard_map/reduce_scatter | solution.py:152
  382.0 8.0 %copy-start.1 = (bf16[512,8192]{1,0:T(8,128)(2,1)S(1)}, bf16[512,8192]{1,0:T(8,128)(2,1)}, u32[]{:S(2)}) copy-start(bf16[512,8192]{1,0:T(8,128)(2,1)} %all-gather.9.cloned.1.call-done) | copy-start | bytes 25165828
Sparse Core Ops, SparseCore 0:
  32.7 25.9 all-gather.12
  60.4 23.3 all-gather.10
  165.3 32.1 all-gather.6
  207.6 92.5 all-reduce.2
  331.0 50.9 all-gather.8
  436.8 92.3 reduce-scatter.4
